TPU v7x, 32 devices: a whole 2x2x4 slice. The times are simulated.
32 devices in a mesh: ctx: 4 (over y, x), pair: 4 (over z), dp: 2 (over core).
Axes of the slice: x: 2, y: 2, z: 4, core: 2. Of those that a mesh axis runs over, the one named last changes fastest.
Arguments:
- queries: bfloat16 [8, 4, 128, 2048], P(('dp', 'ctx'), 'pair'), parts along dimension 0, may hold values from -8 to 8
- resp_keys: bfloat16 [8, 4, 128, 1024], P(('dp', 'ctx'), 'pair'), parts along dimension 0, may hold values from -6 to 6
- resp_values: bfloat16 [8, 4, 128, 1024], P(('dp', 'ctx'), 'pair'), parts along dimension 0, may hold values from -6 to 6
- d_out: bfloat16 [8, 4, 128, 2048], P(('dp', 'ctx'), 'pair'), parts along dimension 0, may hold values from -6 to 6
- prefix_kv: bfloat16 [4, 512, 2, 1024], P('dp', 'ctx', None, 'pair'), parts along dimension 0, may hold values from -8 to 8
- prefix_blocks: int32 [8, 4, 4], P(('dp', 'ctx'), 'pair'), parts along dimension 0, may hold values 0 or 1
- resp_lengths: int32 [8, 4], P(('dp', 'ctx'), 'pair'), parts along dimension 0, may hold values from 32 to 128, as said below
- pair_prompt: int32 [8], P('dp'), parts along dimension 0, may hold values from 0 to 1, as said below
Outputs:
- d_queries: bfloat16 [8, 4, 128, 2048], P(('dp', 'ctx'), 'pair'), parts along dimension 0
- d_resp_keys: bfloat16 [8, 4, 128, 1024], P(('dp', 'ctx'), 'pair'), parts along dimension 0
- d_resp_values: bfloat16 [8, 4, 128, 1024], P(('dp', 'ctx'), 'pair'), parts along dimension 0
- d_prefix: float32 [4, 512, 2, 1024], P('dp', 'ctx', None, 'pair'), parts along dimension 0
There are 2 independent parts, one for each index of `dp`. A program takes and returns all parts, laid end to end along the dimension named above; each array names one. Nothing has to cross between parts.
Inputs may be any that keep to these rules, and one draw needn't show every extreme that they name: `pair_prompt`: each prompt is answered by exactly two indices of pair, one chosen and one rejected response. `resp_lengths`: some response fills all 128 slots.
All inputs are finite; a program needn't handle non-finite values. No bound on the sum of `prefix_blocks` on one device may be relied on, other than what follows from the above.
Results may differ from a plain program's by a relative error of at most 0.012.
The roundings to bfloat16 on the way count: a program that leaves them out, or rounds other values in their place, can miss the bound.
Values may be sent and summed in bfloat16 or wider, within the bound.
No kernel may reach another device: no remote copies, remote signals or barrier semaphores. Data moves between devices by JAX's collectives and lax.ppermute only.
A program may use at most 128 MiB of HBM per device.

v0:
```python
import jax
import jax.numpy as jnp
from jax import lax
from jax.sharding import PartitionSpec as P

KV_HEADS = 8
GROUP = 2
HEAD_DIM = 128
BLOCK = 128
scale_factor = 144.0 ** (-0.5)
neg_big = -1e30


def gather_rows(kv_part):
    return lax.all_gather(kv_part, "ctx", axis=1, tiled=True)


def pick_prompt(kv_part, pair_prompt):
    outgoing = jnp.take(kv_part, pair_prompt, axis=0)
    return lax.all_to_all(outgoing, "pair", split_axis=0, concat_axis=3, tiled=True)


def shards(
    queries, resp_keys, resp_values, d_out, prefix_kv, prefix_blocks, resp_lengths, pair_prompt
):
    prefix_panel = gather_rows(pick_prompt(prefix_kv, pair_prompt))
    prefix_panel = prefix_panel[0]
    resp_rows = queries.shape[2]
    pre_rows = prefix_panel.shape[0]
    n_prompts = prefix_kv.shape[0]
    all_rows = pre_rows + resp_rows
    keys_heads = jnp.transpose(
        jnp.concatenate([prefix_panel[:, 0], resp_keys[0, 0]], 0).reshape(
            all_rows, KV_HEADS, HEAD_DIM
        ),
        (1, 0, 2),
    )
    values_heads = jnp.transpose(
        jnp.concatenate([prefix_panel[:, 1], resp_values[0, 0]], 0).reshape(
            all_rows, KV_HEADS, HEAD_DIM
        ),
        (1, 0, 2),
    )
    query_heads = jnp.transpose(
        queries[0, 0].reshape(resp_rows, KV_HEADS, GROUP, HEAD_DIM), (1, 2, 0, 3)
    )
    positions = jnp.arange(resp_rows, dtype=jnp.int32)
    live_rows = positions < resp_lengths[0, 0]
    grad_rows = jnp.where(live_rows[:, None], d_out[0, 0], jnp.zeros_like(d_out[0, 0]))
    grad_heads = jnp.transpose(
        grad_rows.reshape(resp_rows, KV_HEADS, GROUP, HEAD_DIM), (1, 2, 0, 3)
    )
    visible = prefix_blocks[0, 0] > 0
    prefix_mask = jnp.broadcast_to(visible[:, None], (pre_rows // BLOCK, BLOCK)).reshape(pre_rows)
    causal = positions[:, None] >= positions[None, :]
    allowed = jnp.concatenate(
        [jnp.broadcast_to(prefix_mask[None, :], (resp_rows, pre_rows)), causal], 1
    )

    def one_head(items):
        key_rows, value_rows, query_rows, grad_part = items
        scores = (
            jnp.einsum("jqd,kd->jqk", query_rows, key_rows, preferred_element_type=jnp.float32)
            * scale_factor
        )
        scores = jnp.where(allowed[None], scores, neg_big)
        row_peak = jnp.max(scores, axis=-1, keepdims=True)
        raised = jnp.exp(scores - row_peak)
        weights = raised / jnp.sum(raised, axis=-1, keepdims=True)
        probs_low = weights.astype(jnp.bfloat16)
        attended = jnp.einsum(
            "jqk,kd->jqd", probs_low, value_rows, preferred_element_type=jnp.float32
        )
        attended = lax.optimization_barrier(attended.astype(jnp.bfloat16)).astype(jnp.float32)
        row_delta = jnp.sum(grad_part.astype(jnp.float32) * attended, axis=-1)
        d_probs = jnp.einsum(
            "jqd,kd->jqk", grad_part, value_rows, preferred_element_type=jnp.float32
        )
        ds_low = (weights * (d_probs - row_delta[..., None])).astype(jnp.bfloat16)
        query_grad = (
            jnp.einsum("jqk,kd->jqd", ds_low, key_rows, preferred_element_type=jnp.float32)
            * scale_factor
        )
        key_grad = (
            jnp.einsum("jqk,jqd->kd", ds_low, query_rows, preferred_element_type=jnp.float32)
            * scale_factor
        )
        value_grad = jnp.einsum(
            "jqk,jqd->kd", probs_low, grad_part, preferred_element_type=jnp.float32
        )
        both_grads = jnp.stack([key_grad, value_grad], 1).astype(jnp.bfloat16)
        return (query_grad.astype(jnp.bfloat16), both_grads)

    query_grads, kv_grads = lax.map(one_head, (keys_heads, values_heads, query_heads, grad_heads))
    d_queries = jnp.transpose(query_grads, (2, 0, 1, 3)).reshape(1, 1, resp_rows, -1)
    own_grads = jnp.transpose(kv_grads[:, pre_rows:], (1, 2, 0, 3)).reshape(resp_rows, 2, -1)
    d_resp_keys = own_grads[:, 0].reshape(1, 1, resp_rows, -1)
    d_resp_values = own_grads[:, 1].reshape(1, 1, resp_rows, -1)
    prefix_part = jnp.transpose(kv_grads[:, :pre_rows], (1, 2, 0, 3)).reshape(1, pre_rows, 2, -1)
    pieces = lax.all_to_all(prefix_part, "ctx", split_axis=1, concat_axis=0, tiled=True)
    ctx_total = jnp.sum(pieces.astype(jnp.float32), axis=0).astype(jnp.bfloat16)
    arrived = lax.all_to_all(ctx_total[None], "pair", split_axis=3, concat_axis=0, tiled=True)
    prompt_hits = (pair_prompt[:, None] == jnp.arange(n_prompts, dtype=jnp.int32)[None, :]).astype(
        jnp.float32
    )
    d_prefix = jnp.sum(
        prompt_hits[:, :, None, None, None] * arrived.astype(jnp.float32)[:, None], axis=0
    )
    return (d_queries, d_resp_keys, d_resp_values, d_prefix)


def solution(mesh):
    placed = (
        P(("dp", "ctx"), "pair", None, None),
        P(("dp", "ctx"), "pair", None, None),
        P(("dp", "ctx"), "pair", None, None),
        P(("dp", "ctx"), "pair", None, None),
        P("dp", "ctx", None, "pair"),
        P(("dp", "ctx"), "pair", None),
        P(("dp", "ctx"), "pair"),
        P("dp"),
    )
    return jax.shard_map(
        shards,
        mesh=mesh,
        in_specs=placed,
        out_specs=(
            P(("dp", "ctx"), "pair", None, None),
            P(("dp", "ctx"), "pair", None, None),
            P(("dp", "ctx"), "pair", None, None),
            P("dp", "ctx", None, "pair"),
        ),
        check_vma=False,
    )
```

profile of v0, /device:TPU:0, one launch (start us, length us, event | category | flops | bytes accessed | tf_op | source)
XLA Modules:
  0.0 192.6 jit_solution(804473975615161115)
XLA Ops:
  8.6 1.6 gather_fusion
  10.8 20.7 %all_to_all.39 = bf16[4,128,2,256]{3,2,1,0:T(2,128)(2,1)S(1)} all-to-all(bf16[4,128,2,256]{3,2,1,0:T(2,128)(2,1)S(1)} %broadcast_select_fusion), channel_id=1, replica_groups=mesh['ctx'=4,'pair'=4,'dp'=2] {'pair'}, dimensions={0} | all-to-all | bytes 1048576 | tf_op jit(solution)/shard_map/all_to_all | solution.py:20
  35.3 31.8 %all-gather.2.cloned.1.call-done = bf16[1,512,2,1024]{1,3,2,0:T(8,128)(2,1)} async-done(((bf16[1,128,2,1024]{1,3,2,0:T(8,128)(2,1)}), bf16[1,512,2,1024]{1,3,2,0:T(8,128)(2,1)}) %all-gather.2.cloned.1.call-update) | async-done | bytes 2097168 | tf_op jit(solution)/shard_map/all_gather | solution.py:15
  67.1 1.7 fusion.55
  68.7 1.3 maximum_bitcast_fusion
  70.1 50.9 %while.12 = (s32[]{:T(128)}, bf16[8,2,128,128]{3,2,1,0:T(8,128)(2,1)}, bf16[8,640,2,128]{3,1,2,0:T(8,128)(2,1)}, pred[128,640]{1,0:T(8,128)(4,1)S(1)}, bf16[8,2,...) while((s32[]{:T(128)}, ...), condition=%wide.region_4.5_spmd, body=%wide.region_0.4_spmd.sunk | while | flops 254427520 | bytes 6446201 | solution.py:94
  70.1 1.4 fusion.90
  73.3 1.8 fusion.93
  76.4 1.4 fusion.90
  79.6 1.8 fusion.93
  82.8 1.4 fusion.90
  86.0 1.8 fusion.93
  89.1 1.4 fusion.90
  92.4 1.8 fusion.93
  95.5 1.4 fusion.90
  98.7 1.8 fusion.93
  101.9 1.4 fusion.90
  105.1 1.8 fusion.93
  108.2 1.4 fusion.90
  111.4 1.8 fusion.93
  114.6 1.4 fusion.90
  117.8 1.8 fusion.93
  121.0 3.2 %copy.93 = bf16[8,640,2,128]{1,3,0,2:T(8,128)(2,1)S(1)} copy(bf16[8,640,2,128]{3,1,2,0:T(8,128)(2,1)} %get-tuple-element.48) | data formatting | bytes 5242880 | tf_op jit(solution)/shard_map/while | solution.py:94
  124.1 1.5 slice.30
  125.7 6.2 %copy.94 = bf16[1,512,2,1024]{3,2,0,1:T(2,128)(2,1)} copy(bf16[1,512,2,1024]{1,3,2,0:T(8,128)(2,1)} %bitcast.153) | data formatting | bytes 4194304 | tf_op jit(solution)/shard_map/reshape | solution.py:99
  131.9 29.2 %all_to_all.40 = bf16[1,512,2,1024]{3,2,0,1:T(2,128)(2,1)S(1)} all-to-all(bf16[1,512,2,1024]{3,2,0,1:T(2,128)(2,1)} %copy.94), channel_id=1, replica_groups=mesh['ctx'=4,'pair'=4,'dp'=2] {'ctx'}, dimensions={1} | all-to-all | bytes 4194304 | tf_op jit(solution)/shard_map/all_to_all | solution.py:100
  161.1 3.1 %reduce_sum.39 = bf16[128,2,1024]{2,1,0:T(2,128)(2,1)S(1)} reduce(bf16[4,128,2,1024]{3,2,1,0:T(2,128)(2,1)S(1)} %bitcast.152, bf16[]{:T(256)} %constant.29.clone.1), dimensions={0}, to_apply=%region_5.6 | reduce | flops 786432 | bytes 2621442 | tf_op jit(solution)/shard_map/reduce_sum | solution.py:101
  164.2 1.9 copy.95
  166.1 4.6 %all-to-all-start.2 = ((bf16[1,128,2,1024]{1,2,0,3:T(2,128)(2,1)}), bf16[1,128,2,1024]{1,2,0,3:T(2,128)(2,1)S(1)}, u32[]{:S(2)}, u32[]{:S(2)}) async-start(bf16[1,128,2,1024]{1,2,0,3:T(2,128)(2,1)} %copy.95), calls=%async_computation.2 | async-start | bytes 1048576 | tf_op jit(solution)/shard_map/all_to_all | solution.py:102
  171.3 1.2 reshape.115
  174.5 9.3 %all-to-all-done.2 = bf16[1,128,2,1024]{1,2,0,3:T(2,128)(2,1)S(1)} async-done(((bf16[1,128,2,1024]{1,2,0,3:T(2,128)(2,1)}), bf16[1,128,2,1024]{1,2,0,3:T(2,128)(2,1)S(1)}, u32[]{:S(2)}, u32[]{:S(2)}) %all-to-all-start.2) | async-done | bytes 524320 | tf_op jit(solution)/shard_map/all_to_all | solution.py:102
  184.5 1.2 copy.98
  (116 shorter events, 33.0 us)
Async XLA Ops:
  7.2 1.4 copy-start
  7.2 59.9 %all-gather.2.cloned.1.call-start = ((), (), s32[]{:S(2)}) async-start(), calls=%async_computation.3 | async-start | bytes 2621440 | tf_op jit(solution)/shard_map/all_gather | solution.py:15
  10.2 22.4 %copy-start.1 = (bf16[1,1,128,2048]{3,2,1,0:T(8,128)(2,1)S(1)}, bf16[1,1,128,2048]{3,2,1,0:T(8,128)(2,1)}, u32[]{:S(2)}) copy-start(bf16[1,1,128,2048]{3,2,1,0:T(8,128)(2,1)} %param.10) | copy-start | bytes 1572868
  10.7 22.2 %copy-start.4 = (bf16[1,1,128,1024]{3,2,1,0:T(8,128)(2,1)S(1)}, bf16[1,1,128,1024]{3,2,1,0:T(8,128)(2,1)}, u32[]{:S(2)}) copy-start(bf16[1,1,128,1024]{3,2,1,0:T(8,128)(2,1)} %param.11) | copy-start | bytes 786436
  10.8 22.4 %copy-start.5 = (bf16[1,1,128,1024]{3,2,1,0:T(8,128)(2,1)S(1)}, bf16[1,1,128,1024]{3,2,1,0:T(8,128)(2,1)}, u32[]{:S(2)}) copy-start(bf16[1,1,128,1024]{3,2,1,0:T(8,128)(2,1)} %param.12) | copy-start | bytes 786436
  31.5 1.8 copy-start.2
  32.6 1.6 copy-start.7
  161.1 9.6 %copy-start.6 = (s32[4]{0:T(128)S(1)}, s32[4]{0:T(128)}, u32[]{:S(2)}) copy-start(s32[4]{0:T(128)} %param.17) | copy-start | bytes 52
  161.1 9.7 %copy-start.3 = (bf16[8,2,128,128]{3,2,1,0:T(8,128)(2,1)S(1)}, bf16[8,2,128,128]{3,2,1,0:T(8,128)(2,1)}, u32[]{:S(2)}) copy-start(bf16[8,2,128,128]{3,2,1,0:T(8,128)(2,1)} %get-tuple-element.47) | copy-start | bytes 1572868
  166.1 17.7 %all-to-all-start.2 = ((bf16[1,128,2,1024]{1,2,0,3:T(2,128)(2,1)}), bf16[1,128,2,1024]{1,2,0,3:T(2,128)(2,1)S(1)}, u32[]{:S(2)}, u32[]{:S(2)}) async-start(bf16[1,128,2,1024]{1,2,0,3:T(2,128)(2,1)} %copy.95), calls=%async_computation.2 | async-start | bytes 1048576 | tf_op jit(solution)/shard_map/all_to_all | solution.py:102
Sparse Core Ops, SparseCore 0:
  32.7 34.2 all-gather.1
where the time goes:
time: 194 us; the launch traced here: 193 us
  blocking collectives  50 us (26%)
  waiting for transfers between devices  41.1 us (21%)
  matrix products  34.8 us (18%)
  local copies, waits for them, and re-layouts  31.2 us (16%)
  other arithmetic  15.5 us (8%)
  between operations  14.9 us (8%)
  starting transfers between devices  4.64 us (2%)
    all_gather x1, waiting for transfers between devices, gather_rows(): return lax.all_gather(kv_part, 'ctx', axis=1, tiled=True)  31.8 us
    all_to_all x1, blocking collectives, shards(): lax.all_to_all(prefix_part, 'ctx', split_axis=1, concat_axis=0, tiled=True)  29.2 us
    all_to_all x1, blocking collectives, pick_prompt(): lax.all_to_all(outgoing, 'pair', split_axis=0, concat_axis=3, tiled=True)  20.7 us
    dot_general x8, matrix products, one_head(): jnp.einsum('jqk,kd->jqd', ds_low, key_rows, preferred_element_type=jnp.fl...  14.4 us
    sub x8, matrix products, one_head(): raised = jnp.exp(scores - row_peak)  11.3 us
    all_to_all x1, waiting for transfers between devices, shards(): lax.all_to_all(ctx_total[None], 'pair', split_axis=3, concat_axis=0, tile...  9.32 us
    dynamic_slice x16, local copies, waits for them, and re-layouts, shards(): lax.map(one_head, (keys_heads, values_heads, query_heads, grad_heads))  7.76 us
    reshape x1, local copies, waits for them, and re-layouts, shards(): jnp.transpose(kv_grads[:, :pre_rows], (1, 2, 0, 3))  6.24 us
  transfers between devices with their start and end apart: 2, of which 2 were waited for; matrix products, arithmetic and copies ran while one was open for 3% of the time, Pallas kernels for 0%

commit v1 on v0

--- a/solution.py
+++ b/solution.py
@@ -1,3 +1,4 @@
+import functools
 import jax
 import jax.numpy as jnp
 from jax import lax
@@ -11,8 +12,28 @@
 neg_big = -1e30
 
 
+def do_spots(xs, a_name):
+    found_now = lax.psum(1, axis_name=a_name)
+    q_next, y1, heard = (found_now, lax.axis_index(a_name), xs.shape[1])
+    next_value, spare = (xs, 1)
+    while spare < q_next:
+        tray = []
+        b = 0
+        while b < q_next:
+            tray.append((b, (b - spare) % q_next))
+            b = b + 1
+        block_next = lax.ppermute(next_value, axis_name=a_name, perm=tray)
+        next_value = jnp.concatenate([next_value, block_next], axis=1)
+        spare = 2 * spare
+    local_out = jnp.roll(next_value, y1 * heard, axis=1)
+    return local_out
+
+
+see_the_layers_all = functools.partial(do_spots, a_name="ctx")
+
+
 def gather_rows(kv_part):
-    return lax.all_gather(kv_part, "ctx", axis=1, tiled=True)
+    return see_the_layers_all(kv_part)
 
 
 def pick_prompt(kv_part, pair_prompt):

time: 194 us -> 178 us (0.918)
  between operations: 14.9 us -> 1.55 us
  waiting for transfers between devices: 41.1 us -> 32.2 us
  starting transfers between devices: 4.64 us -> 8.74 us
  local copies, waits for them, and re-layouts: 31.2 us -> 34.5 us
  blocking collectives: 50 us -> 47.7 us
    all_gather x1 -> x0, waiting for transfers between devices: 31.8 us -> none  [gather_rows(): return lax.all_gather(kv_part, 'ctx', axis=1, tiled=True)]
    ppermute x0 -> x2, waiting for transfers between devices: none -> 26.3 us  [do_spots(): block_next = lax.ppermute(next_value, axis_name=a_name, perm=tray)]
    unnamed x21 -> x26, local copies, waits for them, and re-layouts: 2.12 us -> 6.18 us
    ppermute x0 -> x2, starting transfers between devices: none -> 4.02 us  [do_spots(): block_next = lax.ppermute(next_value, axis_name=a_name, perm=tray)]
    all_to_all x1, waiting for transfers between devices: 9.32 us -> 5.84 us  [shards(): lax.all_to_all(ctx_total[None], 'pair', split_axis=3, concat_axis=0, tile...]
    all_to_all x1, blocking collectives: 29.2 us -> 27 us  [shards(): lax.all_to_all(prefix_part, 'ctx', split_axis=1, concat_axis=0, tiled=True)]
  transfers between devices with their start and end apart: 2 -> 3, of which waited for: 2 -> 3; matrix products, arithmetic and copies ran while one was open for 3% -> 5% of each run, Pallas kernels for 0% -> 0%
where the time goes in v1:
time: 178 us; the launch traced here: 177 us
  blocking collectives  47.7 us (27%)
  matrix products  34.8 us (20%)
  local copies, waits for them, and re-layouts  34.5 us (19%)
  waiting for transfers between devices  32.2 us (18%)
  other arithmetic  16.7 us (9%)
  starting transfers between devices  8.74 us (5%)
    all_to_all x1, blocking collectives, shards(): lax.all_to_all(prefix_part, 'ctx', split_axis=1, concat_axis=0, tiled=True)  27 us
    ppermute x2, waiting for transfers between devices, do_spots(): block_next = lax.ppermute(next_value, axis_name=a_name, perm=tray)  26.3 us
    all_to_all x1, blocking collectives, pick_prompt(): lax.all_to_all(outgoing, 'pair', split_axis=0, concat_axis=3, tiled=True)  20.7 us
    dot_general x8, matrix products, one_head(): jnp.einsum('jqk,kd->jqd', ds_low, key_rows, preferred_element_type=jnp.fl...  14.4 us
    sub x8, matrix products, one_head(): raised = jnp.exp(scores - row_peak)  11.3 us
    dynamic_slice x16, local copies, waits for them, and re-layouts, shards(): lax.map(one_head, (keys_heads, values_heads, query_heads, grad_heads))  7.75 us
    reshape x1, local copies, waits for them, and re-layouts, shards(): jnp.transpose(kv_grads[:, :pre_rows], (1, 2, 0, 3))  6.26 us
    unnamed x26, local copies, waits for them, and re-layouts  6.18 us
  transfers between devices with their start and end apart: 3, of which 3 were waited for; matrix products, arithmetic and copies ran while one was open for 5% of the time, Pallas kernels for 0%

profile of v1, /device:TPU:0, one launch (start us, length us, event | category | flops | bytes accessed | tf_op | source)
XLA Modules:
  0.0 176.5 jit_solution(12557780135112569436)
XLA Ops:
  2.0 1.6 gather_fusion
  4.2 20.7 %all_to_all.39 = bf16[4,128,2,256]{3,2,1,0:T(2,128)(2,1)S(1)} all-to-all(bf16[4,128,2,256]{3,2,1,0:T(2,128)(2,1)S(1)} %broadcast_select_fusion), channel_id=1, replica_groups=mesh['ctx'=4,'pair'=4,'dp'=2] {'pair'}, dimensions={0} | all-to-all | bytes 1048576 | tf_op jit(solution)/shard_map/all_to_all | solution.py:41
  25.4 2.5 %collective-permute-start = (bf16[1,128,2,1024]{1,3,2,0:T(8,128)(2,1)S(1)}, bf16[1,128,2,1024]{1,3,2,0:T(8,128)(2,1)S(1)}, u32[]{:S(2)}, u32[]{:S(2)}) collective-permute-start(bf16[1,128,2,1024]{1,3,2,0:T(8,128)(2,1)S(1)} %bitcast.155), channel_id=1, source_target_pairs={{0,24},{8,0},{16,8},{24,16},{1,25},{9,1},{17,9},{25,17},{2,26},{10... | collective-permute-start | bytes 1572872 | tf_op jit(solution)/shard_map/ppermute | solution.py:25
  27.9 10.1 %collective-permute-done = bf16[1,128,2,1024]{1,3,2,0:T(8,128)(2,1)S(1)} collective-permute-done((bf16[1,128,2,1024]{1,3,2,0:T(8,128)(2,1)S(1)}, bf16[1,128,2,1024]{1,3,2,0:T(8,128)(2,1)S(1)}, u32[]{:S(2)}, u32[]{:S(2)}) %collective-permute-start) | collective-permute-done | bytes 524320 | tf_op jit(solution)/shard_map/ppermute | solution.py:25
  39.1 1.5 collective-permute-start.1
  45.9 16.3 %collective-permute-done.1 = bf16[1,256,2,1024]{1,3,2,0:T(8,128)(2,1)S(1)} collective-permute-done((bf16[1,256,2,1024]{1,3,2,0:T(8,128)(2,1)}, bf16[1,256,2,1024]{1,3,2,0:T(8,128)(2,1)S(1)}, u32[]{:S(2)}, u32[]{:S(2)}) %collective-permute-start.1) | collective-permute-done | bytes 1048608 | tf_op jit(solution)/shard_map/ppermute | solution.py:25
  65.5 50.8 %while.12 = (s32[]{:T(128)}, bf16[8,2,128,128]{3,2,1,0:T(8,128)(2,1)}, bf16[8,640,2,128]{3,1,2,0:T(8,128)(2,1)}, pred[128,640]{1,0:T(8,128)(4,1)S(1)}, bf16[8,2,...) while((s32[]{:T(128)}, ...), condition=%wide.region_4.5_spmd, body=%wide.region_0.4_spmd.sunk | while | flops 254427520 | bytes 6446701 | solution.py:115
  65.5 1.4 fusion.90
  70.0 1.8 %fusion.93 = bf16[8,2,128,128]{3,2,1,0:T(8,128)(2,1)} fusion(bf16[8,2,128,128]{3,2,1,0:T(8,128)(2,1)} %get-tuple-element.180, s32[]{:T(128)} %get-tuple-element.179, bf16[2,128,640]{2,1,0:T(8,128)(2,1)S(1)} %fusion.92, bf16[8,640,128]{1,2,0:T(8,128)(2,1)} %get-tuple-element.193), kind=kOutput, calls=%fused_computation.20.clone.1 | convolution fusion | flops 42008576 | bytes 558080 | tf_op jit(solution)/shard_map/while/body/eval_jaxpr/jqk,kd->jqd/dot_general | solution.py:102
  71.8 1.4 fusion.90
  76.4 1.8 %fusion.93 = bf16[8,2,128,128]{3,2,1,0:T(8,128)(2,1)} fusion(bf16[8,2,128,128]{3,2,1,0:T(8,128)(2,1)} %get-tuple-element.180, s32[]{:T(128)} %get-tuple-element.179, bf16[2,128,640]{2,1,0:T(8,128)(2,1)S(1)} %fusion.92, bf16[8,640,128]{1,2,0:T(8,128)(2,1)} %get-tuple-element.193), kind=kOutput, calls=%fused_computation.20.clone.1 | convolution fusion | flops 42008576 | bytes 558080 | tf_op jit(solution)/shard_map/while/body/eval_jaxpr/jqk,kd->jqd/dot_general | solution.py:102
  78.2 1.4 fusion.90
  82.7 1.8 %fusion.93 = bf16[8,2,128,128]{3,2,1,0:T(8,128)(2,1)} fusion(bf16[8,2,128,128]{3,2,1,0:T(8,128)(2,1)} %get-tuple-element.180, s32[]{:T(128)} %get-tuple-element.179, bf16[2,128,640]{2,1,0:T(8,128)(2,1)S(1)} %fusion.92, bf16[8,640,128]{1,2,0:T(8,128)(2,1)} %get-tuple-element.193), kind=kOutput, calls=%fused_computation.20.clone.1 | convolution fusion | flops 42008576 | bytes 558080 | tf_op jit(solution)/shard_map/while/body/eval_jaxpr/jqk,kd->jqd/dot_general | solution.py:102
  84.5 1.4 fusion.90
  89.1 1.8 %fusion.93 = bf16[8,2,128,128]{3,2,1,0:T(8,128)(2,1)} fusion(bf16[8,2,128,128]{3,2,1,0:T(8,128)(2,1)} %get-tuple-element.180, s32[]{:T(128)} %get-tuple-element.179, bf16[2,128,640]{2,1,0:T(8,128)(2,1)S(1)} %fusion.92, bf16[8,640,128]{1,2,0:T(8,128)(2,1)} %get-tuple-element.193), kind=kOutput, calls=%fused_computation.20.clone.1 | convolution fusion | flops 42008576 | bytes 558080 | tf_op jit(solution)/shard_map/while/body/eval_jaxpr/jqk,kd->jqd/dot_general | solution.py:102
  90.9 1.4 fusion.90
  95.4 1.8 %fusion.93 = bf16[8,2,128,128]{3,2,1,0:T(8,128)(2,1)} fusion(bf16[8,2,128,128]{3,2,1,0:T(8,128)(2,1)} %get-tuple-element.180, s32[]{:T(128)} %get-tuple-element.179, bf16[2,128,640]{2,1,0:T(8,128)(2,1)S(1)} %fusion.92, bf16[8,640,128]{1,2,0:T(8,128)(2,1)} %get-tuple-element.193), kind=kOutput, calls=%fused_computation.20.clone.1 | convolution fusion | flops 42008576 | bytes 558080 | tf_op jit(solution)/shard_map/while/body/eval_jaxpr/jqk,kd->jqd/dot_general | solution.py:102
  97.2 1.4 fusion.90
  101.8 1.8 %fusion.93 = bf16[8,2,128,128]{3,2,1,0:T(8,128)(2,1)} fusion(bf16[8,2,128,128]{3,2,1,0:T(8,128)(2,1)} %get-tuple-element.180, s32[]{:T(128)} %get-tuple-element.179, bf16[2,128,640]{2,1,0:T(8,128)(2,1)S(1)} %fusion.92, bf16[8,640,128]{1,2,0:T(8,128)(2,1)} %get-tuple-element.193), kind=kOutput, calls=%fused_computation.20.clone.1 | convolution fusion | flops 42008576 | bytes 558080 | tf_op jit(solution)/shard_map/while/body/eval_jaxpr/jqk,kd->jqd/dot_general | solution.py:102
  103.6 1.4 fusion.90
  108.2 1.8 %fusion.93 = bf16[8,2,128,128]{3,2,1,0:T(8,128)(2,1)} fusion(bf16[8,2,128,128]{3,2,1,0:T(8,128)(2,1)} %get-tuple-element.180, s32[]{:T(128)} %get-tuple-element.179, bf16[2,128,640]{2,1,0:T(8,128)(2,1)S(1)} %fusion.92, bf16[8,640,128]{1,2,0:T(8,128)(2,1)} %get-tuple-element.193), kind=kOutput, calls=%fused_computation.20.clone.1 | convolution fusion | flops 42008576 | bytes 558080 | tf_op jit(solution)/shard_map/while/body/eval_jaxpr/jqk,kd->jqd/dot_general | solution.py:102
  109.9 1.4 fusion.90
  114.5 1.8 %fusion.93 = bf16[8,2,128,128]{3,2,1,0:T(8,128)(2,1)} fusion(bf16[8,2,128,128]{3,2,1,0:T(8,128)(2,1)} %get-tuple-element.180, s32[]{:T(128)} %get-tuple-element.179, bf16[2,128,640]{2,1,0:T(8,128)(2,1)S(1)} %fusion.92, bf16[8,640,128]{1,2,0:T(8,128)(2,1)} %get-tuple-element.193), kind=kOutput, calls=%fused_computation.20.clone.1 | convolution fusion | flops 42008576 | bytes 558080 | tf_op jit(solution)/shard_map/while/body/eval_jaxpr/jqk,kd->jqd/dot_general | solution.py:102
  116.3 3.2 %copy.93 = bf16[8,640,2,128]{1,3,0,2:T(8,128)(2,1)S(1)} copy(bf16[8,640,2,128]{3,1,2,0:T(8,128)(2,1)} %get-tuple-element.48) | data formatting | bytes 5242880 | tf_op jit(solution)/shard_map/while | solution.py:115
  119.5 1.5 slice.30
  121.0 6.3 %copy.94 = bf16[1,512,2,1024]{3,2,0,1:T(2,128)(2,1)} copy(bf16[1,512,2,1024]{1,3,2,0:T(8,128)(2,1)} %bitcast.154) | data formatting | bytes 4194304 | tf_op jit(solution)/shard_map/reshape | solution.py:120
  127.2 27.0 %all_to_all.40 = bf16[1,512,2,1024]{3,2,0,1:T(2,128)(2,1)S(1)} all-to-all(bf16[1,512,2,1024]{3,2,0,1:T(2,128)(2,1)} %copy.94), channel_id=1, replica_groups=mesh['ctx'=4,'pair'=4,'dp'=2] {'ctx'}, dimensions={1} | all-to-all | bytes 4194304 | tf_op jit(solution)/shard_map/all_to_all | solution.py:121
  154.2 3.1 %reduce_sum.39 = bf16[128,2,1024]{2,1,0:T(2,128)(2,1)S(1)} reduce(bf16[4,128,2,1024]{3,2,1,0:T(2,128)(2,1)S(1)} %bitcast.153, bf16[]{:T(256)} %constant.68.clone.1), dimensions={0}, to_apply=%region_5.6 | reduce | flops 786432 | bytes 2621442 | tf_op jit(solution)/shard_map/reduce_sum | solution.py:122
  157.3 1.9 %copy.95 = bf16[1,128,2,1024]{1,2,0,3:T(2,128)(2,1)} copy(bf16[1,128,2,1024]{3,2,1,0:T(2,128)(2,1)S(1)} %bitcast.164) | data formatting | bytes 1048576 | tf_op jit(solution)/shard_map/broadcast_in_dim | solution.py:123
  159.2 4.7 %all-to-all-start.2 = ((bf16[1,128,2,1024]{1,2,0,3:T(2,128)(2,1)}), bf16[1,128,2,1024]{1,2,0,3:T(2,128)(2,1)S(1)}, u32[]{:S(2)}, u32[]{:S(2)}) async-start(bf16[1,128,2,1024]{1,2,0,3:T(2,128)(2,1)} %copy.95), calls=%async_computation.2 | async-start | bytes 1048576 | tf_op jit(solution)/shard_map/all_to_all | solution.py:123
  164.0 1.6 copy.91
  168.7 5.8 %all-to-all-done.2 = bf16[1,128,2,1024]{1,2,0,3:T(2,128)(2,1)S(1)} async-done(((bf16[1,128,2,1024]{1,2,0,3:T(2,128)(2,1)}), bf16[1,128,2,1024]{1,2,0,3:T(2,128)(2,1)S(1)}, u32[]{:S(2)}, u32[]{:S(2)}) %all-to-all-start.2) | async-done | bytes 524320 | tf_op jit(solution)/shard_map/all_to_all | solution.py:123
  (125 shorter events, 41.1 us)
Async XLA Ops:
  0.6 1.4 copy-start
  0.6 27.3 %copy-start.7 = (s32[1,1,4]{2,1,0:T(1,128)S(1)}, s32[1,1,4]{2,1,0:T(1,128)}, u32[]{:S(2)}) copy-start(s32[1,1,4]{2,1,0:T(1,128)} %param.15) | copy-start | bytes 52
  3.6 37.1 %copy-start.4 = (bf16[1,1,128,1024]{3,2,1,0:T(8,128)(2,1)S(1)}, bf16[1,1,128,1024]{3,2,1,0:T(8,128)(2,1)}, u32[]{:S(2)}) copy-start(bf16[1,1,128,1024]{3,2,1,0:T(8,128)(2,1)} %param.11) | copy-start | bytes 786436
  4.2 37.4 %copy-start.5 = (bf16[1,1,128,1024]{3,2,1,0:T(8,128)(2,1)S(1)}, bf16[1,1,128,1024]{3,2,1,0:T(8,128)(2,1)}, u32[]{:S(2)}) copy-start(bf16[1,1,128,1024]{3,2,1,0:T(8,128)(2,1)} %param.12) | copy-start | bytes 786436
  4.2 38.2 %copy-start.3 = (bf16[1,1,128,2048]{3,2,1,0:T(8,128)(2,1)S(1)}, bf16[1,1,128,2048]{3,2,1,0:T(8,128)(2,1)}, u32[]{:S(2)}) copy-start(bf16[1,1,128,2048]{3,2,1,0:T(8,128)(2,1)} %param.13) | copy-start | bytes 1572868
  25.4 12.6 %collective-permute-start = (bf16[1,128,2,1024]{1,3,2,0:T(8,128)(2,1)S(1)}, bf16[1,128,2,1024]{1,3,2,0:T(8,128)(2,1)S(1)}, u32[]{:S(2)}, u32[]{:S(2)}) collective-permute-start(bf16[1,128,2,1024]{1,3,2,0:T(8,128)(2,1)S(1)} %bitcast.155), channel_id=1, source_target_pairs={{0,24},{8,0},{16,8},{24,16},{1,25},{9,1},{17,9},{25,17},{2,26},{10... | collective-permute-start | bytes 1572872 | tf_op jit(solution)/shard_map/ppermute | solution.py:25
  39.1 23.1 %collective-permute-start.1 = (bf16[1,256,2,1024]{1,3,2,0:T(8,128)(2,1)}, bf16[1,256,2,1024]{1,3,2,0:T(8,128)(2,1)S(1)}, u32[]{:S(2)}, u32[]{:S(2)}) collective-permute-start(bf16[1,256,2,1024]{1,3,2,0:T(8,128)(2,1)} %pad_maximum_fusion), channel_id=1, source_target_pairs={{0,16},{8,24},{16,0},{24,8},{1,17},{9,25},{17,1},{25,9},{2,18},{10... | collective-permute-start | bytes 3145736 | tf_op jit(solution)/shard_map/ppermute | solution.py:25
  63.1 1.0 copy-start.1
  63.1 1.0 copy-start.2
  154.2 9.7 %copy-start.6 = (s32[4]{0:T(128)S(1)}, s32[4]{0:T(128)}, u32[]{:S(2)}) copy-start(s32[4]{0:T(128)} %param.17) | copy-start | bytes 52
  159.2 15.3 %all-to-all-start.2 = ((bf16[1,128,2,1024]{1,2,0,3:T(2,128)(2,1)}), bf16[1,128,2,1024]{1,2,0,3:T(2,128)(2,1)S(1)}, u32[]{:S(2)}, u32[]{:S(2)}) async-start(bf16[1,128,2,1024]{1,2,0,3:T(2,128)(2,1)} %copy.95), calls=%async_computation.2 | async-start | bytes 1048576 | tf_op jit(solution)/shard_map/all_to_all | solution.py:123
